TPU v7x, 256 devices: a whole 4x4x8 slice. The times are simulated.
256 devices in a mesh: tm: 32 (over y, x, core), tensor: 8 (over z).
Axes of the slice: x: 4, y: 4, z: 8, core: 2. Of those that a mesh axis runs over, the one named last changes fastest.
Arguments:
- features: bfloat16 [32768, 1536], P(('tm', 'tensor')), may hold values from -4 to 4
- frame_mask: int32 [32768], P('tm'), may hold values 0 or 1
- total_length: int32 [1], replicated, may hold values from 24576 to 32768
- norm_gain: float32 [1536], replicated, may hold values from 0.1 to 1.9
- value_weight: bfloat16 [1536, 1536], P(None, 'tensor'), may hold values from -0.15625 to 0.15625
- gate_weight: bfloat16 [1536, 1536], P(None, 'tensor'), may hold values from -0.15625 to 0.15625
- depth_kernel: float32 [31, 1536], P(None, 'tensor'), may hold values from -1 to 1
- batch_gain: float32 [1536], P('tensor'), may hold values from 0.1 to 1.9
- batch_bias: float32 [1536], P('tensor'), may hold values from -2 to 2
- out_weight: bfloat16 [1536, 1536], P('tensor'), may hold values from -0.15625 to 0.15625
- feed_gain: float32 [1536], replicated, may hold values from 0.1 to 1.9
- up_weight: bfloat16 [1536, 6144], P('tm', 'tensor'), may hold values from -0.15625 to 0.15625
- down_weight: bfloat16 [6144, 1536], P('tensor', 'tm'), may hold values from -0.078125 to 0.078125
Outputs:
- encoded: bfloat16 [32768, 1536], P(('tm', 'tensor'))
All inputs are finite; a program needn't handle non-finite values. No bound on the sum of `frame_mask` on one device may be relied on, other than what follows from the above.
Results may differ from a plain program's by a relative error of at most 0.0074.
Values may be sent and summed in bfloat16 or wider, within the bound.
No kernel may reach another device: no remote copies, remote signals or barrier semaphores. Data moves between devices by JAX's collectives and lax.ppermute only.
A program may use at most 64 MiB of HBM per device.

v0:
```python
import jax
import jax.numpy as jnp
from jax import lax
from jax.sharding import PartitionSpec as P

KERNEL = 31


def extended(array, sides, width):
    for axis, dim in sides:
        devices, length = (lax.axis_size(axis), array.shape[dim])
        up = [(i, (i + 1) % devices) for i in range(devices - 1)]
        down = [(j, i) for i, j in up]
        last = lax.slice_in_dim(array, length - width, length, axis=dim)
        initial = lax.slice_in_dim(array, 0, width, axis=dim)
        before = lax.ppermute(last, axis, up)
        after = lax.ppermute(initial, axis, down)
        array = jnp.concatenate([before, array, after], axis=dim)
    return array


def layer_norm(rows, gain):
    values = rows.astype(jnp.float32)
    centre = jnp.mean(values, axis=-1, keepdims=True)
    spread = jnp.mean(jnp.square(values - centre), axis=-1, keepdims=True)
    return (values - centre) * lax.rsqrt(spread + 1e-05) * gain


def merge_moments(low, high):
    n_a, mean_a, m2_a = (low[0], low[1], low[2])
    n_b, mean_b, m2_b = (high[0], high[1], high[2])
    n = n_a + n_b
    share = jnp.where(n > 0, n_b / jnp.maximum(n, 1.0), 0.0)
    delta = mean_b - mean_a
    mean = mean_a + delta * share
    m2 = m2_a + m2_b + jnp.square(delta) * n_a * share
    return jnp.stack([n, mean, m2])


def moments_over(stats, axis):
    size = lax.axis_size(axis)
    me = lax.axis_index(axis)
    step = 1
    while step < size:
        pairs = [(i, i ^ step) for i in range(size)]
        other = lax.ppermute(stats, axis, pairs)
        mine_low = me & step == 0
        low = jnp.where(mine_low, stats, other)
        high = jnp.where(mine_low, other, stats)
        stats = merge_moments(low, high)
        step *= 2
    return stats


def shards(
    features,
    frame_mask,
    total_length,
    norm_gain,
    value_weight,
    gate_weight,
    depth_kernel,
    batch_gain,
    batch_bias,
    out_weight,
    feed_gain,
    up_weight,
    down_weight,
):
    own_rows = features.shape[0]
    block = own_rows * lax.axis_size("tensor")
    positions = lax.axis_index("tm") * block + jnp.arange(block, dtype=jnp.int32)
    valid = ((frame_mask > 0) & (positions < total_length[0])).astype(jnp.float32)
    normed = layer_norm(features, norm_gain).astype(jnp.bfloat16)
    piece = lax.all_gather(normed, "tensor", axis=0, tiled=True)
    up_whole = lax.all_gather(up_weight, "tm", axis=0, tiled=True)
    down_whole = lax.all_gather(down_weight, "tm", axis=1, tiled=True)
    value = jnp.dot(piece, value_weight, preferred_element_type=jnp.float32)
    gate = jnp.dot(piece, gate_weight, preferred_element_type=jnp.float32)
    glu = (value * jax.nn.sigmoid(gate) * valid[:, None]).astype(jnp.bfloat16)
    padded = extended(glu, (("tm", 0),), KERNEL // 2)
    conv = jnp.zeros(glu.shape, jnp.float32)
    for tap in range(KERNEL):
        conv = conv + padded[tap : tap + block].astype(jnp.float32) * depth_kernel[tap]
    count_local = jnp.sum(valid)
    local_sum = jnp.sum(conv * valid[:, None], axis=0)
    local_mean = jnp.where(count_local > 0, local_sum / jnp.maximum(count_local, 1.0), 0.0)
    local_m2 = jnp.sum(jnp.square(conv - local_mean) * valid[:, None], axis=0)
    stats = jnp.stack([jnp.broadcast_to(count_local, local_sum.shape), local_mean, local_m2])
    stats = moments_over(stats, "tm")
    count, mean, m2 = (stats[0], stats[1], stats[2])
    centred = conv - mean
    var = m2 / count
    scaled = centred * lax.rsqrt(var + 1e-05) * batch_gain + batch_bias
    swished = (scaled * jax.nn.sigmoid(scaled)).astype(jnp.bfloat16)
    conv_part = jnp.dot(swished, out_weight, preferred_element_type=jnp.float32)
    conv_part, up_whole, down_whole = lax.optimization_barrier((conv_part, up_whole, down_whole))
    conv_out = lax.psum_scatter(
        conv_part.astype(jnp.bfloat16), "tensor", scatter_dimension=0, tiled=True
    ).astype(jnp.float32)
    mid = (features.astype(jnp.float32) + conv_out).astype(jnp.bfloat16)
    feed_normed = layer_norm(mid, feed_gain).astype(jnp.bfloat16)
    feed_block = lax.all_gather(feed_normed, "tensor", axis=0, tiled=True)
    pre = jnp.dot(feed_block, up_whole, preferred_element_type=jnp.float32)
    hidden = (pre * jax.nn.sigmoid(pre)).astype(jnp.bfloat16)
    partial_out = jnp.dot(hidden, down_whole, preferred_element_type=jnp.float32)
    feed_out = lax.psum_scatter(
        partial_out.astype(jnp.bfloat16), "tensor", scatter_dimension=0, tiled=True
    ).astype(jnp.float32)
    return (mid.astype(jnp.float32) + 0.5 * feed_out).astype(jnp.bfloat16)


def solution(mesh):
    placed = (
        P(("tm", "tensor"), None),
        P("tm"),
        P(),
        P(),
        P(None, "tensor"),
        P(None, "tensor"),
        P(None, "tensor"),
        P("tensor"),
        P("tensor"),
        P("tensor", None),
        P(),
        P("tm", "tensor"),
        P("tensor", "tm"),
    )
    return jax.shard_map(
        shards, mesh=mesh, in_specs=placed, out_specs=P(("tm", "tensor"), None), check_vma=False
    )
```

profile of v0, /device:TPU:2, one launch (start us, length us, event | category | flops | bytes accessed | tf_op | source)
XLA Modules:
  0.0 321.7 jit_solution(17575117318898476684)
XLA Ops:
  6.5 1.2 convert_reduce_fusion.1
  7.7 1.2 fusion.13
  9.0 2.0 fusion.15
  11.1 0.7 all-gather.7.cloned.1.call-update
  11.8 0.7 all-gather.9.cloned.1.call-update
  13.2 1.0 fusion.66
  14.3 1.4 fusion.63
  15.6 43.5 %all-gather.5.cloned.1.call-done = bf16[1024,1536]{1,0:T(8,128)(2,1)} async-done(((bf16[128,1536]{1,0:T(8,128)(2,1)}), bf16[1024,1536]{1,0:T(8,128)(2,1)}) %all-gather.5.cloned.1.call-update) | async-done | bytes 3145744 | tf_op jit(solution)/shard_map/all_gather | solution.py:75
  59.1 3.4 %fusion.4 = f32[1024,192]{0,1:T(8,128)S(1)} fusion(bf16[1024,1536]{1,0:T(8,128)(2,1)} %all-gather.5.cloned.1.call-done, bf16[1536,192]{0,1:T(8,128)(2,1)} %param.18), kind=kOutput, calls=%fused_computation.36 | convolution fusion | flops 604569600 | bytes 4521984 | tf_op jit(solution)/shard_map/dot_general | solution.py:79
  62.6 1.2 fusion.5
  63.9 1.9 collective-permute-start
  65.8 3.6 %collective-permute-start.1 = (bf16[15,192]{0,1:T(8,128)(2,1)S(1)}, bf16[15,192]{0,1:T(8,128)(2,1)S(1)}, u32[]{:S(2)}, u32[]{:S(2)}) collective-permute-start(bf16[15,192]{0,1:T(8,128)(2,1)S(1)} %get-tuple-element.32), channel_id=1, source_target_pairs={{8,0},{16,8},{24,16},{32,24},{40,32},{48,40},{56,48},{64,56},{72,6... | collective-permute-start | bytes 17288 | tf_op jit(solution)/shard_map/ppermute | solution.py:17
  69.4 1.0 fusion.67
  72.4 5.6 %multiply_reduce_fusion.1 = (f32[192]{0:T(256)S(1)}, f32[1024,192]{0,1:T(8,128)S(1)}) fusion(f32[1024]{0:T(1024)S(1)} %get-tuple-element.28, f32[192]{0:T(256)S(1)} %bitcast.79, bf16[15,192]{0,1:T(8,128)(2,1)S(1)} %collective-permute-done.1, bf16[1024,192]{0,1:T(8,128)(2,1)S(1)} %fusion.5, f32[192]{0:T(256)S(1)} %bitcast.80, f32[192]{0:T(256)S(1)} %bitcast.51, ...), kind=kLoop, calls=%fused_computation.58 | loop fusion | flops 36175680 | bytes 1219840 | tf_op jit(solution)/shard_map/reduce_sum | solution.py:86
  78.7 0.8 collective-permute-done.2
  80.3 3.1 collective-permute-done.3
  83.5 4.3 %collective-permute-start.4 = (f32[3,192]{1,0:T(4,128)S(1)}, f32[3,192]{1,0:T(4,128)S(1)}, u32[]{:S(2)}, u32[]{:S(2)}) collective-permute-start(f32[3,192]{1,0:T(4,128)S(1)} %pad_maximum_fusion.4), channel_id=1, source_target_pairs={{0,32},{8,40},{16,48},{24,56},{32,0},{40,8},{48,16},{56,24},{64,96... | collective-permute-start | bytes 6920 | tf_op jit(solution)/shard_map/ppermute | solution.py:46
  87.7 1.6 collective-permute-done.4
  89.4 1.6 collective-permute-start.5
  91.0 2.1 collective-permute-done.5
  93.2 3.2 collective-permute-start.6
  96.4 2.3 collective-permute-done.6
  98.7 2.9 fusion.18
  101.6 7.7 %all-gather.7.cloned.1.call-done = bf16[1536,768]{1,0:T(8,128)(2,1)} async-done(((bf16[48,768]{1,0:T(8,128)(2,1)}), bf16[1536,768]{1,0:T(8,128)(2,1)}) %all-gather.7.cloned.1.call-update) | async-done | bytes 2359312 | tf_op jit(solution)/shard_map/all_gather | solution.py:76
  109.3 51.2 %all-gather.9.cloned.1.call-done = bf16[768,1536]{0,1:T(8,128)(2,1)} async-done(((bf16[768,48]{0,1:T(8,128)(2,1)}), bf16[768,1536]{0,1:T(8,128)(2,1)}) %all-gather.9.cloned.1.call-update) | async-done | bytes 2359312 | tf_op jit(solution)/shard_map/all_gather | solution.py:77
  160.6 48.8 %reduce-scatter.3.cloned.1.call-done = bf16[128,1536]{1,0:T(8,128)(2,1)} async-done(((bf16[1024,1536]{1,0:T(8,128)(2,1)}), bf16[128,1536]{1,0:T(8,128)(2,1)}) %reduce-scatter.3.cloned.1.call-update) | async-done | bytes 393232 | tf_op jit(solution)/shard_map/reduce_scatter | solution.py:98
  209.3 1.2 convert_reduce_fusion
  210.8 1.0 fusion.12
  211.9 44.4 %all-gather.11.cloned.1.call-done = bf16[1024,1536]{1,0:T(8,128)(2,1)} async-done(((bf16[128,1536]{1,0:T(8,128)(2,1)}), bf16[1024,1536]{1,0:T(8,128)(2,1)}) %all-gather.11.cloned.1.call-update) | async-done | bytes 3145744 | tf_op jit(solution)/shard_map/all_gather | solution.py:103
  256.4 11.1 %convolution_convert_fusion = bf16[1024,1536]{1,0:T(8,128)(2,1)} fusion(bf16[768,1536]{0,1:T(8,128)(2,1)} %all-gather.9.cloned.1.call-done, bf16[1024,1536]{1,0:T(8,128)(2,1)} %all-gather.11.cloned.1.call-done, bf16[1536,768]{1,0:T(8,128)(2,1)} %all-gather.7.cloned.1.call-done), kind=kOutput, calls=%fused_computation | convolution fusion | flops 4837343232 | bytes 11010048 | tf_op jit(solution)/shard_map/dot_general | solution.py:106
  267.4 45.6 %reduce-scatter.5.cloned.1.call-done = bf16[128,1536]{1,0:T(8,128)(2,1)} async-done(((bf16[1024,1536]{1,0:T(8,128)(2,1)}), bf16[128,1536]{1,0:T(8,128)(2,1)}) %reduce-scatter.5.cloned.1.call-update) | async-done | bytes 393232 | tf_op jit(solution)/shard_map/reduce_scatter | solution.py:107
  313.0 1.9 fusion.17
  (57 shorter events, 3.0 us)
Async XLA Ops:
  6.5 92.2 %copy-start = (bf16[192,1536]{1,0:T(8,128)(2,1)S(1)}, bf16[192,1536]{1,0:T(8,128)(2,1)}, u32[]{:S(2)}) copy-start(bf16[192,1536]{1,0:T(8,128)(2,1)} %param.22) | copy-start | bytes 1769476
  6.5 52.6 %all-gather.5.cloned.1.call-start = ((), (), s32[]{:S(2)}) async-start(), calls=%async_computation.2 | async-start | bytes 3538944 | tf_op jit(solution)/shard_map/all_gather | solution.py:75
  11.1 98.3 %all-gather.7.cloned.1.call-start = ((), (), s32[]{:S(2)}) async-start(), calls=%async_computation.3 | async-start | bytes 2433024 | tf_op jit(solution)/shard_map/all_gather | solution.py:76
  11.8 148.7 %all-gather.9.cloned.1.call-start = ((), (), s32[]{:S(2)}) async-start(), calls=%async_computation.4 | async-start | bytes 2433024 | tf_op jit(solution)/shard_map/all_gather | solution.py:77
  12.5 196.8 %reduce-scatter.3.cloned.1.call-start = ((), (), s32[]{:S(2)}) async-start(), calls=%async_computation.5 | async-start | bytes 3538944 | tf_op jit(solution)/shard_map/reduce_scatter | solution.py:98
  15.6 46.9 %copy-start.4 = (bf16[1536,192]{0,1:T(8,128)(2,1)S(1)}, bf16[1536,192]{0,1:T(8,128)(2,1)}, u32[]{:S(2)}) copy-start(bf16[1536,192]{0,1:T(8,128)(2,1)} %param.17) | copy-start | bytes 1769476
  59.1 3.4 %copy-start.3 = (bf16[1024,1536]{1,0:T(8,128)(2,1)S(1)}, bf16[1024,1536]{1,0:T(8,128)(2,1)}, u32[]{:S(2)}) copy-start(bf16[1024,1536]{1,0:T(8,128)(2,1)} %all-gather.5.cloned.1.call-done) | copy-start | bytes 9437188
  62.6 36.1 %copy-start.5 = (f32[192]{0:T(256)S(1)}, f32[192]{0:T(256)}, u32[]{:S(2)}) copy-start(f32[192]{0:T(256)} %param.21) | copy-start | bytes 2308
  62.6 36.1 %copy-start.6 = (f32[192]{0:T(256)S(1)}, f32[192]{0:T(256)}, u32[]{:S(2)}) copy-start(f32[192]{0:T(256)} %param.20) | copy-start | bytes 2308
  63.9 8.5 %collective-permute-start = (bf16[15,192]{0,1:T(8,128)(2,1)S(1)}, bf16[15,192]{0,1:T(8,128)(2,1)S(1)}, u32[]{:S(2)}, u32[]{:S(2)}) collective-permute-start(bf16[15,192]{0,1:T(8,128)(2,1)S(1)} %get-tuple-element.31), channel_id=1, source_target_pairs={{0,8},{8,16},{16,24},{24,32},{32,40},{40,48},{48,56},{56,64},{64,7... | collective-permute-start | bytes 17288 | tf_op jit(solution)/shard_map/ppermute | solution.py:16
  65.8 6.6 %collective-permute-start.1 = (bf16[15,192]{0,1:T(8,128)(2,1)S(1)}, bf16[15,192]{0,1:T(8,128)(2,1)S(1)}, u32[]{:S(2)}, u32[]{:S(2)}) collective-permute-start(bf16[15,192]{0,1:T(8,128)(2,1)S(1)} %get-tuple-element.32), channel_id=1, source_target_pairs={{8,0},{16,8},{24,16},{32,24},{40,32},{48,40},{56,48},{64,56},{72,6... | collective-permute-start | bytes 17288 | tf_op jit(solution)/shard_map/ppermute | solution.py:17
  78.3 1.2 collective-permute-start.2
  79.7 3.7 %collective-permute-start.3 = (f32[3,192]{1,0:T(4,128)S(1)}, f32[3,192]{1,0:T(4,128)S(1)}, u32[]{:S(2)}, u32[]{:S(2)}) collective-permute-start(f32[3,192]{1,0:T(4,128)S(1)} %pad_maximum_fusion.3), channel_id=1, source_target_pairs={{0,16},{8,24},{16,0},{24,8},{32,48},{40,56},{48,32},{56,40},{64,80... | collective-permute-start | bytes 6920 | tf_op jit(solution)/shard_map/ppermute | solution.py:46
  83.5 5.9 %collective-permute-start.4 = (f32[3,192]{1,0:T(4,128)S(1)}, f32[3,192]{1,0:T(4,128)S(1)}, u32[]{:S(2)}, u32[]{:S(2)}) collective-permute-start(f32[3,192]{1,0:T(4,128)S(1)} %pad_maximum_fusion.4), channel_id=1, source_target_pairs={{0,32},{8,40},{16,48},{24,56},{32,0},{40,8},{48,16},{56,24},{64,96... | collective-permute-start | bytes 6920 | tf_op jit(solution)/shard_map/ppermute | solution.py:46
  89.4 3.7 %collective-permute-start.5 = (f32[3,192]{1,0:T(4,128)S(1)}, f32[3,192]{1,0:T(4,128)S(1)}, u32[]{:S(2)}, u32[]{:S(2)}) collective-permute-start(f32[3,192]{1,0:T(4,128)S(1)} %pad_maximum_fusion.5), channel_id=1, source_target_pairs={{0,64},{8,72},{16,80},{24,88},{32,96},{40,104},{48,112},{56,120},{... | collective-permute-start | bytes 6920 | tf_op jit(solution)/shard_map/ppermute | solution.py:46
  93.2 5.5 %collective-permute-start.6 = (f32[3,192]{1,0:T(4,128)S(1)}, f32[3,192]{1,0:T(4,128)S(1)}, u32[]{:S(2)}, u32[]{:S(2)}) collective-permute-start(f32[3,192]{1,0:T(4,128)S(1)} %pad_maximum_fusion.6), channel_id=1, source_target_pairs={{0,128},{8,136},{16,144},{24,152},{32,160},{40,168},{48,176},{56,1... | collective-permute-start | bytes 6920 | tf_op jit(solution)/shard_map/ppermute | solution.py:46
  101.6 107.8 %copy-start.1 = (bf16[128,1536]{1,0:T(8,128)(2,1)S(1)}, bf16[128,1536]{1,0:T(8,128)(2,1)}, u32[]{:S(2)}) copy-start(bf16[128,1536]{1,0:T(8,128)(2,1)} %param.13) | copy-start | bytes 1179652
  101.6 109.2 %copy-start.2 = (f32[1536]{0:T(1024)S(1)}, f32[1536]{0:T(1024)}, u32[]{:S(2)}) copy-start(f32[1536]{0:T(1024)} %param.23) | copy-start | bytes 18436
  160.5 95.9 %all-gather.11.cloned.1.call-start = ((), (), s32[]{:S(2)}) async-start(), calls=%async_computation.6 | async-start | bytes 3538944 | tf_op jit(solution)/shard_map/all_gather | solution.py:103
  211.9 101.1 %reduce-scatter.5.cloned.1.call-start = ((), (), s32[]{:S(2)}) async-start(), calls=%async_computation.7 | async-start | bytes 3538944 | tf_op jit(solution)/shard_map/reduce_scatter | solution.py:107
Sparse Core Ops, SparseCore 0:
  11.2 47.9 all-gather.4
  61.7 47.5 all-gather.6
  111.8 48.5 all-gather.8
  162.9 46.4 reduce-scatter.2
  212.0 44.3 all-gather.10
  267.6 45.4 reduce-scatter.4
where the time goes:
time: 322 us
  waiting for transfers between devices  253 us (79%)
  matrix products  18.5 us (6%)
  other arithmetic  16.4 us (5%)
  starting transfers between devices  15.9 us (5%)
  between operations  15.7 us (5%)
    all_gather x1, waiting for transfers between devices, shards(): down_whole = lax.all_gather(down_weight, 'tm', axis=1, tiled=True)  51.2 us
    reduce_scatter x1, waiting for transfers between devices, shards(): lax.psum_scatter(conv_part.astype(jnp.bfloat16), 'tensor', scatter_dimens...  48.8 us
    reduce_scatter x1, waiting for transfers between devices, shards(): lax.psum_scatter(partial_out.astype(jnp.bfloat16), 'tensor', scatter_dime...  45.6 us
    all_gather x1, waiting for transfers between devices, shards(): feed_block = lax.all_gather(feed_normed, 'tensor', axis=0, tiled=True)  44.4 us
    all_gather x1, waiting for transfers between devices, shards(): piece = lax.all_gather(normed, 'tensor', axis=0, tiled=True)  43.5 us
    dot_general x1, matrix products, shards(): jnp.dot(hidden, down_whole, preferred_element_type=jnp.float32)  11.1 us
    ppermute x5, starting transfers between devices, moments_over(): other = lax.ppermute(stats, axis, pairs)  10.1 us
    ppermute x5, waiting for transfers between devices, moments_over(): other = lax.ppermute(stats, axis, pairs)  9.85 us
  transfers between devices with their start and end apart: 13, of which 11 were waited for; matrix products, arithmetic and copies ran while one was open for 6% of the time, Pallas kernels for 0%

commit v1 on v0

--- a/solution.py
+++ b/solution.py
@@ -4,6 +4,12 @@
 from jax.sharding import PartitionSpec as P
 
 KERNEL = 31
+
+
+def gather_from_all(x, axis, dim):
+    devices = lax.axis_size(axis)
+    repeats = [devices if d == dim else 1 for d in range(x.ndim)]
+    return lax.all_to_all(jnp.tile(x, repeats), axis, split_axis=dim, concat_axis=dim, tiled=True)
 
 
 def extended(array, sides, width):
@@ -72,7 +78,7 @@
     positions = lax.axis_index("tm") * block + jnp.arange(block, dtype=jnp.int32)
     valid = ((frame_mask > 0) & (positions < total_length[0])).astype(jnp.float32)
     normed = layer_norm(features, norm_gain).astype(jnp.bfloat16)
-    piece = lax.all_gather(normed, "tensor", axis=0, tiled=True)
+    piece = gather_from_all(normed, "tensor", 0)
     up_whole = lax.all_gather(up_weight, "tm", axis=0, tiled=True)
     down_whole = lax.all_gather(down_weight, "tm", axis=1, tiled=True)
     value = jnp.dot(piece, value_weight, preferred_element_type=jnp.float32)

time: 322 us -> 296 us (0.919)
  waiting for transfers between devices: 253 us -> 216 us
  starting transfers between devices: 15.9 us -> 25.4 us
    all_to_all x0 -> x1, waiting for transfers between devices: none -> 71 us  [gather_from_all(): lax.all_to_all(jnp.tile(x, repeats), axis, split_axis=dim, concat_axis=di...]
    all_gather x1, waiting for transfers between devices: 51.2 us -> 0.01 us  [shards(): down_whole = lax.all_gather(down_weight, 'tm', axis=1, tiled=True)]
    all_gather x1 -> x0, waiting for transfers between devices: 43.5 us -> none  [shards(): piece = lax.all_gather(normed, 'tensor', axis=0, tiled=True)]
    all_to_all x0 -> x1, starting transfers between devices: none -> 8.6 us  [gather_from_all(): lax.all_to_all(jnp.tile(x, repeats), axis, split_axis=dim, concat_axis=di...]
    all_gather x1, waiting for transfers between devices: 7.71 us -> 0.01 us  [shards(): up_whole = lax.all_gather(up_weight, 'tm', axis=0, tiled=True)]
    reduce_scatter x1, waiting for transfers between devices: 48.8 us -> 44 us  [shards(): lax.psum_scatter(conv_part.astype(jnp.bfloat16), 'tensor', scatter_dimens...]
  transfers between devices with their start and end apart: 13 -> 13, of which waited for: 11 -> 9; matrix products, arithmetic and copies ran while one was open for 6% -> 6% of each run, Pallas kernels for 0% -> 0%
where the time goes in v1:
time: 296 us; the launch traced here: 295 us
  waiting for transfers between devices  216 us (73%)
  starting transfers between devices  25.4 us (9%)
  matrix products  20.2 us (7%)
  between operations  15.4 us (5%)
  other arithmetic  15 us (5%)
    all_to_all x1, waiting for transfers between devices, gather_from_all(): lax.all_to_all(jnp.tile(x, repeats), axis, split_axis=dim, concat_axis=di...  71 us
    reduce_scatter x1, waiting for transfers between devices, shards(): lax.psum_scatter(partial_out.astype(jnp.bfloat16), 'tensor', scatter_dime...  45.6 us
    all_gather x1, waiting for transfers between devices, shards(): feed_block = lax.all_gather(feed_normed, 'tensor', axis=0, tiled=True)  44.6 us
    reduce_scatter x1, waiting for transfers between devices, shards(): lax.psum_scatter(conv_part.astype(jnp.bfloat16), 'tensor', scatter_dimens...  44 us
    ppermute x5, starting transfers between devices, moments_over(): other = lax.ppermute(stats, axis, pairs)  11.1 us
    dot_general x1, matrix products, shards(): jnp.dot(hidden, down_whole, preferred_element_type=jnp.float32)  11 us
    ppermute x5, waiting for transfers between devices, moments_over(): other = lax.ppermute(stats, axis, pairs)  9.72 us
    all_to_all x1, starting transfers between devices, gather_from_all(): lax.all_to_all(jnp.tile(x, repeats), axis, split_axis=dim, concat_axis=di...  8.6 us
  transfers between devices with their start and end apart: 13, of which 9 were waited for; matrix products, arithmetic and copies ran while one was open for 6% of the time, Pallas kernels for 0%

profile of v1, /device:TPU:2, one launch (start us, length us, event | category | flops | bytes accessed | tf_op | source)
XLA Modules:
  0.0 295.1 jit_solution(12547482134063443312)
XLA Ops:
  6.5 1.2 convert_reduce_fusion.1
  7.7 1.2 fusion.13
  9.0 1.3 fusion.15
  10.3 1.9 tile.2
  12.2 8.6 %all-to-all-start = ((bf16[8,128,1536]{2,1,0:T(8,128)(2,1)}), bf16[8,128,1536]{2,1,0:T(8,128)(2,1)}, u32[]{:S(2)}, u32[]{:S(2)}) async-start(bf16[8,128,1536]{2,1,0:T(8,128)(2,1)} %tile.2), calls=%async_computation | async-start | bytes 6291456 | tf_op jit(solution)/shard_map/all_to_all | solution.py:12
  20.9 0.7 all-gather.4.cloned.1.call-update
  21.6 0.7 all-gather.6.cloned.1.call-update
  23.0 0.7 fusion.63
  23.7 71.0 %all-to-all-done = bf16[8,128,1536]{2,1,0:T(8,128)(2,1)} async-done(((bf16[8,128,1536]{2,1,0:T(8,128)(2,1)}), bf16[8,128,1536]{2,1,0:T(8,128)(2,1)}, u32[]{:S(2)}, u32[]{:S(2)}) %all-to-all-start) | async-done | bytes 3145760 | tf_op jit(solution)/shard_map/all_to_all | solution.py:12
  94.7 3.2 %fusion.4 = f32[1024,192]{0,1:T(8,128)S(1)} fusion(bf16[1024,1536]{1,0:T(8,128)(2,1)} %bitcast, bf16[1536,192]{0,1:T(8,128)(2,1)S(1)} %copy-done.5), kind=kOutput, calls=%fused_computation.36 | convolution fusion | flops 604569600 | bytes 4521984 | tf_op jit(solution)/shard_map/dot_general | solution.py:85
  97.9 3.1 %fusion.5 = bf16[1024,192]{0,1:T(8,128)(2,1)S(1)} fusion(f32[1024,192]{0,1:T(8,128)S(1)} %fusion.4, bf16[1024,1536]{1,0:T(8,128)(2,1)} %bitcast, bf16[1536,192]{0,1:T(8,128)(2,1)S(1)} %copy-done.6, f32[1024]{0:T(1024)S(1)} %get-tuple-element.28), kind=kOutput, calls=%fused_computation.37 | convolution fusion | flops 604569600 | bytes 4919296 | tf_op jit(solution)/shard_map/dot_general | solution.py:84
  101.1 1.9 collective-permute-start
  103.1 3.6 %collective-permute-start.1 = (bf16[15,192]{0,1:T(8,128)(2,1)S(1)}, bf16[15,192]{0,1:T(8,128)(2,1)S(1)}, u32[]{:S(2)}, u32[]{:S(2)}) collective-permute-start(bf16[15,192]{0,1:T(8,128)(2,1)S(1)} %get-tuple-element.32), channel_id=1, source_target_pairs={{8,0},{16,8},{24,16},{32,24},{40,32},{48,40},{56,48},{64,56},{72,6... | collective-permute-start | bytes 17288 | tf_op jit(solution)/shard_map/ppermute | solution.py:23
  108.1 0.7 pad.12.clone
  108.8 5.6 %multiply_reduce_fusion.1 = (f32[192]{0:T(256)S(1)}, f32[1024,192]{0,1:T(8,128)S(1)}) fusion(f32[1024]{0:T(1024)S(1)} %get-tuple-element.28, f32[192]{0:T(256)S(1)} %bitcast.80, bf16[15,192]{0,1:T(8,128)(2,1)S(1)} %collective-permute-done.1, bf16[1024,192]{0,1:T(8,128)(2,1)S(1)} %fusion.5, f32[192]{0:T(256)S(1)} %bitcast.81, f32[192]{0:T(256)S(1)} %bitcast.52, ...), kind=kLoop, calls=%fused_computation.58 | loop fusion | flops 36175680 | bytes 1219840 | tf_op jit(solution)/shard_map/reduce_sum | solution.py:92
  114.7 1.3 collective-permute-start.2
  116.0 0.8 collective-permute-done.2
  117.6 3.1 %collective-permute-done.3 = f32[3,192]{1,0:T(4,128)S(1)} collective-permute-done((f32[3,192]{1,0:T(4,128)S(1)}, f32[3,192]{1,0:T(4,128)S(1)}, u32[]{:S(2)}, u32[]{:S(2)}) %collective-permute-start.3) | collective-permute-done | bytes 2336 | tf_op jit(solution)/shard_map/ppermute | solution.py:52
  120.7 4.3 %collective-permute-start.4 = (f32[3,192]{1,0:T(4,128)S(1)}, f32[3,192]{1,0:T(4,128)S(1)}, u32[]{:S(2)}, u32[]{:S(2)}) collective-permute-start(f32[3,192]{1,0:T(4,128)S(1)} %pad_maximum_fusion.4), channel_id=1, source_target_pairs={{0,32},{8,40},{16,48},{24,56},{32,0},{40,8},{48,16},{56,24},{64,96... | collective-permute-start | bytes 6920 | tf_op jit(solution)/shard_map/ppermute | solution.py:52
  125.1 1.6 collective-permute-done.4
  126.7 1.7 collective-permute-start.5
  128.4 2.0 collective-permute-done.5
  130.5 3.2 %collective-permute-start.6 = (f32[3,192]{1,0:T(4,128)S(1)}, f32[3,192]{1,0:T(4,128)S(1)}, u32[]{:S(2)}, u32[]{:S(2)}) collective-permute-start(f32[3,192]{1,0:T(4,128)S(1)} %pad_maximum_fusion.6), channel_id=1, source_target_pairs={{0,128},{8,136},{16,144},{24,152},{32,160},{40,168},{48,176},{56,1... | collective-permute-start | bytes 6920 | tf_op jit(solution)/shard_map/ppermute | solution.py:52
  133.7 2.2 collective-permute-done.6
  136.0 2.9 fusion.18
  138.9 44.0 %reduce-scatter.3.cloned.1.call-done = bf16[128,1536]{1,0:T(8,128)(2,1)} async-done(((bf16[1024,1536]{1,0:T(8,128)(2,1)}), bf16[128,1536]{1,0:T(8,128)(2,1)}) %reduce-scatter.3.cloned.1.call-update) | async-done | bytes 393232 | tf_op jit(solution)/shard_map/reduce_scatter | solution.py:104
  182.9 1.2 convert_reduce_fusion
  184.4 1.0 fusion.12
  185.5 44.6 %all-gather.8.cloned.1.call-done = bf16[1024,1536]{1,0:T(8,128)(2,1)} async-done(((bf16[128,1536]{1,0:T(8,128)(2,1)}), bf16[1024,1536]{1,0:T(8,128)(2,1)}) %all-gather.8.cloned.1.call-update) | async-done | bytes 3145744 | tf_op jit(solution)/shard_map/all_gather | solution.py:109
  230.0 11.0 %convolution_convert_fusion = bf16[1024,1536]{1,0:T(8,128)(2,1)} fusion(bf16[768,1536]{0,1:T(8,128)(2,1)} %all-gather.6.cloned.1.call-done, bf16[1024,1536]{1,0:T(8,128)(2,1)} %all-gather.8.cloned.1.call-done, bf16[1536,768]{1,0:T(8,128)(2,1)} %all-gather.4.cloned.1.call-done), kind=kOutput, calls=%fused_computation | convolution fusion | flops 4837343232 | bytes 11010048 | tf_op jit(solution)/shard_map/dot_general | solution.py:112
  241.1 45.6 %reduce-scatter.5.cloned.1.call-done = bf16[128,1536]{1,0:T(8,128)(2,1)} async-done(((bf16[1024,1536]{1,0:T(8,128)(2,1)}), bf16[128,1536]{1,0:T(8,128)(2,1)}) %reduce-scatter.5.cloned.1.call-update) | async-done | bytes 393232 | tf_op jit(solution)/shard_map/reduce_scatter | solution.py:113
  286.7 1.9 fusion.17
  (61 shorter events, 1.9 us)
Async XLA Ops:
  6.5 129.4 %copy-start = (bf16[192,1536]{1,0:T(8,128)(2,1)S(1)}, bf16[192,1536]{1,0:T(8,128)(2,1)}, u32[]{:S(2)}) copy-start(bf16[192,1536]{1,0:T(8,128)(2,1)} %param.22) | copy-start | bytes 1769476
  12.2 10.8 %copy-start.4 = (s32[1024]{0:T(1024)S(1)}, s32[1024]{0:T(1024)}, u32[]{:S(2)}) copy-start(s32[1024]{0:T(1024)} %param.14) | copy-start | bytes 12292
  12.2 11.5 %copy-start.2 = (f32[31,192]{1,0:T(8,128)S(1)}, f32[31,192]{1,0:T(8,128)}, u32[]{:S(2)}) copy-start(f32[31,192]{1,0:T(8,128)} %param.19) | copy-start | bytes 71428
  12.2 82.5 %copy-start.5 = (bf16[1536,192]{0,1:T(8,128)(2,1)S(1)}, bf16[1536,192]{0,1:T(8,128)(2,1)}, u32[]{:S(2)}) copy-start(bf16[1536,192]{0,1:T(8,128)(2,1)} %param.18) | copy-start | bytes 1769476
  12.2 82.5 %all-to-all-start = ((bf16[8,128,1536]{2,1,0:T(8,128)(2,1)}), bf16[8,128,1536]{2,1,0:T(8,128)(2,1)}, u32[]{:S(2)}, u32[]{:S(2)}) async-start(bf16[8,128,1536]{2,1,0:T(8,128)(2,1)} %tile.2), calls=%async_computation | async-start | bytes 6291456 | tf_op jit(solution)/shard_map/all_to_all | solution.py:12
  20.8 118.0 %all-gather.4.cloned.1.call-start = ((), (), s32[]{:S(2)}) async-start(), calls=%async_computation.3 | async-start | bytes 2433024 | tf_op jit(solution)/shard_map/all_gather | solution.py:82
  21.6 117.3 %all-gather.6.cloned.1.call-start = ((), (), s32[]{:S(2)}) async-start(), calls=%async_computation.4 | async-start | bytes 2433024 | tf_op jit(solution)/shard_map/all_gather | solution.py:83
  22.3 160.6 %reduce-scatter.3.cloned.1.call-start = ((), (), s32[]{:S(2)}) async-start(), calls=%async_computation.5 | async-start | bytes 3538944 | tf_op jit(solution)/shard_map/reduce_scatter | solution.py:104
  94.7 3.2 %copy-start.6 = (bf16[1536,192]{0,1:T(8,128)(2,1)S(1)}, bf16[1536,192]{0,1:T(8,128)(2,1)}, u32[]{:S(2)}) copy-start(bf16[1536,192]{0,1:T(8,128)(2,1)} %param.17) | copy-start | bytes 1769476
  97.9 38.0 %copy-start.7 = (f32[192]{0:T(256)S(1)}, f32[192]{0:T(256)}, u32[]{:S(2)}) copy-start(f32[192]{0:T(256)} %param.21) | copy-start | bytes 2308
  97.9 38.0 %copy-start.8 = (f32[192]{0:T(256)S(1)}, f32[192]{0:T(256)}, u32[]{:S(2)}) copy-start(f32[192]{0:T(256)} %param.20) | copy-start | bytes 2308
  101.1 7.6 %collective-permute-start = (bf16[15,192]{0,1:T(8,128)(2,1)S(1)}, bf16[15,192]{0,1:T(8,128)(2,1)S(1)}, u32[]{:S(2)}, u32[]{:S(2)}) collective-permute-start(bf16[15,192]{0,1:T(8,128)(2,1)S(1)} %get-tuple-element.31), channel_id=1, source_target_pairs={{0,8},{8,16},{16,24},{24,32},{32,40},{40,48},{48,56},{56,64},{64,7... | collective-permute-start | bytes 17288 | tf_op jit(solution)/shard_map/ppermute | solution.py:22
  103.1 5.7 %collective-permute-start.1 = (bf16[15,192]{0,1:T(8,128)(2,1)S(1)}, bf16[15,192]{0,1:T(8,128)(2,1)S(1)}, u32[]{:S(2)}, u32[]{:S(2)}) collective-permute-start(bf16[15,192]{0,1:T(8,128)(2,1)S(1)} %get-tuple-element.32), channel_id=1, source_target_pairs={{8,0},{16,8},{24,16},{32,24},{40,32},{48,40},{56,48},{64,56},{72,6... | collective-permute-start | bytes 17288 | tf_op jit(solution)/shard_map/ppermute | solution.py:23
  114.7 2.1 collective-permute-start.2
  117.0 3.7 %collective-permute-start.3 = (f32[3,192]{1,0:T(4,128)S(1)}, f32[3,192]{1,0:T(4,128)S(1)}, u32[]{:S(2)}, u32[]{:S(2)}) collective-permute-start(f32[3,192]{1,0:T(4,128)S(1)} %pad_maximum_fusion.3), channel_id=1, source_target_pairs={{0,16},{8,24},{16,0},{24,8},{32,48},{40,56},{48,32},{56,40},{64,80... | collective-permute-start | bytes 6920 | tf_op jit(solution)/shard_map/ppermute | solution.py:52
  120.7 5.9 %collective-permute-start.4 = (f32[3,192]{1,0:T(4,128)S(1)}, f32[3,192]{1,0:T(4,128)S(1)}, u32[]{:S(2)}, u32[]{:S(2)}) collective-permute-start(f32[3,192]{1,0:T(4,128)S(1)} %pad_maximum_fusion.4), channel_id=1, source_target_pairs={{0,32},{8,40},{16,48},{24,56},{32,0},{40,8},{48,16},{56,24},{64,96... | collective-permute-start | bytes 6920 | tf_op jit(solution)/shard_map/ppermute | solution.py:52
  126.7 3.7 %collective-permute-start.5 = (f32[3,192]{1,0:T(4,128)S(1)}, f32[3,192]{1,0:T(4,128)S(1)}, u32[]{:S(2)}, u32[]{:S(2)}) collective-permute-start(f32[3,192]{1,0:T(4,128)S(1)} %pad_maximum_fusion.5), channel_id=1, source_target_pairs={{0,64},{8,72},{16,80},{24,88},{32,96},{40,104},{48,112},{56,120},{... | collective-permute-start | bytes 6920 | tf_op jit(solution)/shard_map/ppermute | solution.py:52
  130.5 5.4 %collective-permute-start.6 = (f32[3,192]{1,0:T(4,128)S(1)}, f32[3,192]{1,0:T(4,128)S(1)}, u32[]{:S(2)}, u32[]{:S(2)}) collective-permute-start(f32[3,192]{1,0:T(4,128)S(1)} %pad_maximum_fusion.6), channel_id=1, source_target_pairs={{0,128},{8,136},{16,144},{24,152},{32,160},{40,168},{48,176},{56,1... | collective-permute-start | bytes 6920 | tf_op jit(solution)/shard_map/ppermute | solution.py:52
  138.8 44.1 %copy-start.1 = (bf16[128,1536]{1,0:T(8,128)(2,1)S(1)}, bf16[128,1536]{1,0:T(8,128)(2,1)}, u32[]{:S(2)}) copy-start(bf16[128,1536]{1,0:T(8,128)(2,1)} %param.13) | copy-start | bytes 1179652
  138.8 45.5 %copy-start.3 = (f32[1536]{0:T(1024)S(1)}, f32[1536]{0:T(1024)}, u32[]{:S(2)}) copy-start(f32[1536]{0:T(1024)} %param.23) | copy-start | bytes 18436
  138.8 91.2 %all-gather.8.cloned.1.call-start = ((), (), s32[]{:S(2)}) async-start(), calls=%async_computation.6 | async-start | bytes 3538944 | tf_op jit(solution)/shard_map/all_gather | solution.py:109
  185.4 101.3 %reduce-scatter.5.cloned.1.call-start = ((), (), s32[]{:S(2)}) async-start(), calls=%async_computation.7 | async-start | bytes 3538944 | tf_op jit(solution)/shard_map/reduce_scatter | solution.py:113
Sparse Core Ops, SparseCore 0:
  24.2 50.4 all-gather.3
  77.2 48.6 all-gather.5
  139.0 43.8 reduce-scatter.2
  185.5 44.4 all-gather.7
  241.2 45.4 reduce-scatter.4
